TPU v7x, 512 devices: a whole 4x4x16 slice. The times are simulated.
512 devices in a mesh: pool: 128 (over x, z, core), tp: 4 (over y).
Axes of the slice: x: 4, y: 4, z: 16, core: 2. Of those that a mesh axis runs over, the one named last changes fastest.
Arguments:
- hidden_rows: bfloat16 [16384, 8192], P('pool', 'tp'), may hold values from -6 to 6
- kv_weight: bfloat16 [8192, 1024], P('tp', 'pool'), may hold values from -0.0625 to 0.0625
- queries: bfloat16 [16384, 4096], P('pool', 'tp'), may hold values from -5 to 5
- cache_table: bfloat16 [1024, 128, 1024], P('pool', None, 'tp'), may hold values from -5 to 5
- retrieval: int32 [128, 64], P('pool'), may hold values from 0 to 1023, as said below
- pattern: int32 [128, 2, 64], P('pool'), may hold values 0 or 1
Outputs:
- attended: bfloat16 [16384, 4096], P('pool', 'tp')
- fresh_kv: bfloat16 [16384, 1024], P('pool', 'tp')
Inputs may be any that keep to these rules, and one draw needn't show every extreme that they name: `retrieval`: each request names 64 blocks held by 64 different devices (block b is held by device b // 8); one device, drawn from the seed, holds a block named by every request.
All inputs are finite; a program needn't handle non-finite values. No bound on the sum of `pattern` on one device may be relied on, other than what follows from the above.
Results may differ from a plain program's by a relative error of at most 0.025.
Values may be sent and summed in bfloat16 or wider, within the bound.
No kernel may reach another device: no remote copies, remote signals or barrier semaphores. Data moves between devices by JAX's collectives and lax.ppermute only.
A program may use at most 192 MiB of HBM per device.

v0:
```python
import math
import jax
import jax.numpy as jnp
import numpy as np
from jax import lax
from jax.sharding import Mesh
from jax.sharding import PartitionSpec as P

HD = 128
QH = 32
KVH = 4
BLK = 128
RBLK = 64
POOL = ("px", "pz", "pc")
ID_SPLIT = 32


def rows_by_keys(left, right):
    return lax.dot_general(
        left, right, (((1,), (1,)), ((), ())), preferred_element_type=jnp.float32
    )


def merge(carry, scores, mask, vals):
    top_now, total_now, numer_now = carry
    top_new = jnp.maximum(top_now, jnp.max(jnp.where(mask, scores, -1e30), axis=1))
    weights_now = jnp.where(mask, jnp.exp(scores - top_new[:, None]), 0.0)
    factor = jnp.exp(top_now - top_new)
    total_new = total_now * factor + jnp.sum(weights_now, axis=1)
    numer_new = numer_now * factor[:, None] + jnp.dot(
        weights_now.astype(jnp.bfloat16), vals, preferred_element_type=jnp.float32
    )
    return (top_new, total_new, numer_new)


def body(hidden_rows, kv_weight, queries, cache_table, retrieval, pattern):
    blocks_dev, blk, width = cache_table.shape
    npool = lax.axis_size(POOL)
    fetch_count = retrieval.shape[1]
    wanted = retrieval[0]
    id_row = jnp.concatenate(
        [
            (wanted // ID_SPLIT).astype(jnp.bfloat16),
            (wanted % ID_SPLIT).astype(jnp.bfloat16),
            jnp.zeros((width - 2 * fetch_count,), jnp.bfloat16),
        ]
    )
    id_block = jnp.broadcast_to(id_row[None, None, :], (1, blk, width))
    outgoing = jnp.concatenate([cache_table, id_block], axis=0)
    nx, nz, nc = (lax.axis_size(a) for a in POOL)
    rows_out = blocks_dev + 1
    step = outgoing.reshape(rows_out, nx, nz, nc, width).transpose(0, 1, 3, 2, 4)
    step = step.reshape(rows_out, nx * nc, nz, width)
    step = lax.all_to_all(step, ("px", "pc"), split_axis=1, concat_axis=1, tiled=True)
    step = lax.all_to_all(step, "pz", split_axis=2, concat_axis=2, tiled=True)
    step = step.reshape(rows_out, nx, nc, nz, width).transpose(1, 3, 2, 0, 4)
    by_token = step.reshape(npool, rows_out, width)
    table = by_token[:, :blocks_dev].reshape(npool * blocks_dev, width)
    id_rows = by_token[:, blocks_dev].astype(jnp.float32)
    wanted_all = (
        id_rows[:, :fetch_count] * ID_SPLIT + id_rows[:, fetch_count : 2 * fetch_count]
    ).astype(jnp.int32)
    picks = (
        wanted_all.reshape(-1)[:, None] == jnp.arange(npool * blocks_dev, dtype=jnp.int32)[None, :]
    ).astype(jnp.bfloat16)
    reply = jnp.dot(picks, table, preferred_element_type=jnp.float32).astype(jnp.bfloat16)
    reply = reply.reshape(npool, fetch_count, 1, width)
    reply, hidden_rows, kv_weight = lax.optimization_barrier((reply, hidden_rows, kv_weight))
    fetched = lax.all_to_all(reply, POOL, split_axis=0, concat_axis=0, tiled=True)
    w_head = lax.all_gather(kv_weight, ("pz", "pc"), axis=1, tiled=True)
    w_all = lax.all_gather(w_head, "px", axis=1, tiled=True)
    partial_kv = jnp.dot(hidden_rows, w_all, preferred_element_type=jnp.float32)
    fresh = lax.psum_scatter(partial_kv.astype(jnp.bfloat16), "tp", scatter_dimension=1, tiled=True)
    count = hidden_rows.shape[0]
    group = QH // KVH
    scale = float(HD) ** (-0.5)
    local_heads = fresh.shape[1] // (2 * HD)
    tokens_step = BLK // math.gcd(BLK, 4)
    steps_count = BLK // tokens_step
    grouped = fetched.reshape(steps_count, tokens_step * fetch_count, width)
    token_of_row = jnp.arange(count * group) // group
    block_of_row = token_of_row // RBLK
    row_pat = jnp.take(pattern[0] != 0, block_of_row, axis=0)
    mask = jnp.tile(row_pat, (1, tokens_step))
    near_mask = token_of_row[:, None] >= jnp.arange(count)[None, :]
    q_heads = queries.reshape(count, local_heads, group * HD)
    q_rows = q_heads[:, 0].reshape(count * group, HD)
    near_keys = fresh[:, 0:HD]
    near_vals = fresh[:, HD : 2 * HD]
    near_scores = rows_by_keys(q_rows, near_keys) * scale
    top = jnp.max(jnp.where(near_mask, near_scores, -1e30), axis=1)
    weights = jnp.where(near_mask, jnp.exp(near_scores - top[:, None]), 0.0)
    total = jnp.sum(weights, axis=1)
    numer = jnp.dot(weights.astype(jnp.bfloat16), near_vals, preferred_element_type=jnp.float32)

    def visit(carry, block_rows):
        keys = block_rows[:, 0:HD]
        vals = block_rows[:, HD : 2 * HD]
        scores = rows_by_keys(q_rows, keys) * scale
        return (merge(carry, scores, mask, vals), None)

    (top, total, numer), unused = lax.scan(visit, (top, total, numer), grouped)
    results = (numer / total[:, None]).reshape(count, group * HD)
    attended = results.astype(jnp.bfloat16)
    return (attended, fresh)


def solution(mesh):
    npool = mesh.shape["pool"]
    ntp = mesh.shape["tp"]
    nx = 4 if npool % 8 == 0 else 1
    fine = Mesh(
        np.asarray(mesh.devices).reshape(nx, npool // (2 * nx), 2, ntp), ("px", "pz", "pc", "tp")
    )
    placed = (
        P(POOL, "tp"),
        P("tp", POOL),
        P(POOL, "tp"),
        P(POOL, None, "tp"),
        P(POOL, None),
        P(POOL, None, None),
    )
    return jax.shard_map(
        body, mesh=fine, in_specs=placed, out_specs=(P(POOL, "tp"), P(POOL, "tp")), check_vma=False
    )
```

profile of v0, /device:TPU:34, one launch (start us, length us, event | category | flops | bytes accessed | tf_op | source)
XLA Modules:
  0.0 318.3 jit_solution(7537971316295151175)
XLA Ops:
  7.2 0.0 copy-start
  7.2 0.7 fusion.32
  7.9 0.1 pad_maximum_fusion.1
  8.0 1.1 pad_maximum_fusion
  9.1 0.2 reshape.149
  9.3 0.1 copy.22
  9.4 14.3 %all_to_all.15 = bf16[9,8,16,256]{3,2,0,1:T(8,128)(2,1)S(1)} all-to-all(bf16[9,8,16,256]{3,2,0,1:T(8,128)(2,1)S(1)} %bitcast.88), channel_id=1, replica_groups=mesh['px'=4,'pz'=16,'pc'=2,'tp'=4] {'px','pc'}, dimensions={1} | all-to-all | bytes 1179648 | tf_op jit(solution)/shard_map/all_to_all | solution.py:54
  23.7 0.2 copy.17
  23.9 49.4 %all_to_all.16 = bf16[9,8,16,256]{3,1,0,2:T(8,128)(2,1)S(1)} all-to-all(bf16[9,8,16,256]{3,1,0,2:T(8,128)(2,1)S(1)} %copy.17), channel_id=1, replica_groups=mesh['px'=4,'pz'=16,'pc'=2,'tp'=4] {'pz'}, dimensions={2} | all-to-all | bytes 1179648 | tf_op jit(solution)/shard_map/all_to_all | solution.py:55
  73.3 0.2 reshape.151
  73.5 0.6 copy.28
  74.1 0.2 reshape.152
  74.4 0.1 fusion.22
  74.5 0.1 eq.17
  74.6 9.2 %fusion.11 = bf16[8192,256]{1,0:T(8,128)(2,1)} fusion(s32[8192]{0:T(1024)S(1)} %eq.17, bf16[128,8,256]{2,0,1:T(8,128)(2,1)S(1)} %slice.39), kind=kOutput, calls=%fused_computation.19 | convolution fusion | flops 4305453056 | bytes 4751360 | tf_op jit(solution)/shard_map/dot_general | solution.py:66
  83.8 0.0 copy-start.2
  83.8 0.0 copy-start.1
  83.8 8.1 %all-to-all-start.2 = ((bf16[128,64,1,256]{3,1,2,0:T(8,128)(2,1)}), bf16[128,64,1,256]{3,1,2,0:T(8,128)(2,1)}, u32[]{:S(2)}, u32[]{:S(2)}) async-start(bf16[128,64,1,256]{3,1,2,0:T(8,128)(2,1)} %bitcast.86), calls=%async_computation.3 | async-start | bytes 8388608 | tf_op jit(solution)/shard_map/all_to_all | solution.py:69
  91.9 0.0 all-gather.3.cloned.1.call-start
  91.9 0.7 all-gather.3.cloned.1.call-update
  92.6 0.0 all-gather.5.cloned.1.call-start
  92.6 91.3 %all-gather.3.cloned.1.call-done = bf16[2048,256]{0,1:T(8,128)(2,1)} async-done(((bf16[2048,8]{0,1:T(8,128)(2,1)}), bf16[2048,256]{0,1:T(8,128)(2,1)}) %all-gather.3.cloned.1.call-update) | async-done | bytes 1048592 | tf_op jit(solution)/shard_map/all_gather | solution.py:70
  183.9 0.0 all-gather.5.cloned.1.call-update
  184.0 0.2 reduce-scatter.2.cloned.1.call-start
  184.2 66.6 %all-gather.5.cloned.1.call-done = bf16[2048,1024]{0,1:T(8,128)(2,1)} async-done(((bf16[2048,256]{0,1:T(8,128)(2,1)}), bf16[2048,1024]{0,1:T(8,128)(2,1)}) %all-gather.5.cloned.1.call-update) | async-done | bytes 4194320 | tf_op jit(solution)/shard_map/all_gather | solution.py:71
  250.8 0.0 copy-done
  250.8 4.4 %convolution_convert_fusion = bf16[128,1024]{1,0:T(8,128)(2,1)} fusion(bf16[128,2048]{1,0:T(8,128)(2,1)S(1)} %copy-done, bf16[2048,1024]{0,1:T(8,128)(2,1)} %all-gather.5.cloned.1.call-done), kind=kOutput, calls=%fused_computation.22 | convolution fusion | flops 537001984 | bytes 4980736 | tf_op jit(solution)/shard_map/dot_general | solution.py:72
  255.2 0.0 reduce-scatter.2.cloned.1.call-update
  255.2 0.0 copy-done.2
  255.3 3.0 gather_fusion
  258.3 0.2 broadcast_select_fusion
  258.5 0.2 copy.21
  258.7 0.0 copy-done.1
  258.7 0.1 reshape_squeeze_reshape.3
  258.9 24.5 %reduce-scatter.2.cloned.1.call-done = bf16[128,256]{1,0:T(8,128)(2,1)} async-done(((bf16[128,1024]{1,0:T(8,128)(2,1)}), bf16[128,256]{1,0:T(8,128)(2,1)}) %reduce-scatter.2.cloned.1.call-update) | async-done | bytes 65552 | tf_op jit(solution)/shard_map/reduce_scatter | solution.py:73
  283.3 1.0 select_reduce_fusion
  284.3 0.1 fusion.16
  284.5 1.0 fusion.17
  285.5 0.6 all-to-all-done.2
  286.1 24.6 %while.15 = (s32[]{:T(128)}, f32[1024]{0:T(1024)S(1)}, f32[1024]{0:T(1024)S(1)}, f32[1024,128]{1,0:T(8,128)S(1)}, bf16[4,2048,256]{2,1,0:T(8,128)(2,1)}, /*index...) while((s32[]{:T(128)}, f32[1024]{0:T(1024)S(1)}, f32[1024]{0:T(1024)S(1)}, ...), condition=%wide.region_6.7_spmd.clone, body=%wide.region_3.6_spmd.clone.sunk | while | flops 1090783232 | bytes 29814880 | solution.py:102
  286.1 1.3 dynamic-slice_bitcast_fusion.2
  287.4 1.3 fusion.47
  288.7 1.9 fusion.48
  290.7 1.5 convolution_add_fusion.2
  292.3 1.3 dynamic-slice_bitcast_fusion.2
  293.6 1.3 fusion.47
  294.9 1.9 fusion.48
  296.9 1.5 convolution_add_fusion.2
  298.4 1.3 dynamic-slice_bitcast_fusion.2
  299.7 1.3 fusion.47
  301.1 1.9 fusion.48
  303.0 1.5 convolution_add_fusion.2
  304.6 1.3 dynamic-slice_bitcast_fusion.2
  305.9 1.3 fusion.47
  307.2 1.9 fusion.48
  309.2 1.5 convolution_add_fusion.2
  310.7 0.2 divide_convert_fusion
  311.0 0.8 convert_element_type.43
  (21 shorter events, 0.2 us)
Async XLA Ops:
  7.2 243.6 %copy-start = (bf16[128,2048]{1,0:T(8,128)(2,1)S(1)}, bf16[128,2048]{1,0:T(8,128)(2,1)}, u32[]{:S(2)}) copy-start(bf16[128,2048]{1,0:T(8,128)(2,1)} %param.8) | copy-start | bytes 1572868
  83.8 171.5 %copy-start.2 = (s32[1,2,64]{2,1,0:T(2,128)S(1)}, s32[1,2,64]{2,1,0:T(2,128)}, u32[]{:S(2)}) copy-start(s32[1,2,64]{2,1,0:T(2,128)} %param.13) | copy-start | bytes 1540
  83.8 175.0 %copy-start.1 = (bf16[128,1024]{1,0:T(8,128)(2,1)S(1)}, bf16[128,1024]{1,0:T(8,128)(2,1)}, u32[]{:S(2)}) copy-start(bf16[128,1024]{1,0:T(8,128)(2,1)} %param.10) | copy-start | bytes 786436
  83.8 202.4 %all-to-all-start.2 = ((bf16[128,64,1,256]{3,1,2,0:T(8,128)(2,1)}), bf16[128,64,1,256]{3,1,2,0:T(8,128)(2,1)}, u32[]{:S(2)}, u32[]{:S(2)}) async-start(bf16[128,64,1,256]{3,1,2,0:T(8,128)(2,1)} %bitcast.86), calls=%async_computation.3 | async-start | bytes 8388608 | tf_op jit(solution)/shard_map/all_to_all | solution.py:69
  91.9 92.1 %all-gather.3.cloned.1.call-start = ((), (), s32[]{:S(2)}) async-start(), calls=%async_computation.4 | async-start | bytes 1081344 | tf_op jit(solution)/shard_map/all_gather | solution.py:70
  92.6 158.2 %all-gather.5.cloned.1.call-start = ((), (), s32[]{:S(2)}) async-start(), calls=%async_computation.5 | async-start | bytes 5242880 | tf_op jit(solution)/shard_map/all_gather | solution.py:71
  184.0 99.4 %reduce-scatter.2.cloned.1.call-start = ((), (), s32[]{:S(2)}) async-start(), calls=%async_computation.6 | async-start | bytes 327680 | tf_op jit(solution)/shard_map/reduce_scatter | solution.py:73
Sparse Core Ops, SparseCore 0:
  94.8 89.0 all-gather.2
  186.0 64.7 all-gather.4
  255.4 27.9 reduce-scatter.1
where the time goes:
time: 319 us; the launch traced here: 318 us
  waiting for transfers between devices  184 us (58%)
  blocking collectives  63.7 us (20%)
  matrix products  27 us (8%)
  between operations  13.9 us (4%)
  local copies, waits for them, and re-layouts  11 us (3%)
  other arithmetic  10.4 us (3%)
  starting transfers between devices  8.39 us (3%)
    all_gather x1, waiting for transfers between devices, body(): w_head = lax.all_gather(kv_weight, ('pz', 'pc'), axis=1, tiled=True)  91.3 us
    all_gather x1, waiting for transfers between devices, body(): w_all = lax.all_gather(w_head, 'px', axis=1, tiled=True)  66.6 us
    all_to_all x1, blocking collectives, body(): step = lax.all_to_all(step, 'pz', split_axis=2, concat_axis=2, tiled=True)  49.4 us
    reduce_scatter x1, waiting for transfers between devices, body(): lax.psum_scatter(partial_kv.astype(jnp.bfloat16), 'tp', scatter_dimension...  24.5 us
    all_to_all x1, blocking collectives, body(): lax.all_to_all(step, ('px', 'pc'), split_axis=1, concat_axis=1, tiled=True)  14.3 us
    dot_general x1, matrix products, body(): jnp.dot(picks, table, preferred_element_type=jnp.float32)  9.18 us
    all_to_all x1, starting transfers between devices, body(): lax.all_to_all(reply, POOL, split_axis=0, concat_axis=0, tiled=True)  8.1 us
    convert_element_type x4, other arithmetic, merge(): weights_now.astype(jnp.bfloat16)  7.79 us
  transfers between devices with their start and end apart: 4, of which 4 were waited for; matrix products, arithmetic and copies ran while one was open for 3% of the time, Pallas kernels for 0%

commit v1 on v0

--- a/solution.py
+++ b/solution.py
@@ -52,7 +52,9 @@
     step = outgoing.reshape(rows_out, nx, nz, nc, width).transpose(0, 1, 3, 2, 4)
     step = step.reshape(rows_out, nx * nc, nz, width)
     step = lax.all_to_all(step, ("px", "pc"), split_axis=1, concat_axis=1, tiled=True)
-    step = lax.all_to_all(step, "pz", split_axis=2, concat_axis=2, tiled=True)
+    pieces = jnp.split(step, lax.axis_size("pz"), axis=2)
+    received = lax.all_to_all(jnp.stack(pieces), "pz", 0, 0)
+    step = jnp.concatenate(received, axis=2)
     step = step.reshape(rows_out, nx, nc, nz, width).transpose(1, 3, 2, 0, 4)
     by_token = step.reshape(npool, rows_out, width)
     table = by_token[:, :blocks_dev].reshape(npool * blocks_dev, width)

time: 319 us -> 320 us (level)
  the two profiles are of different devices: /device:TPU:34 before, /device:TPU:58 now
where the time goes in v1:
time: 320 us; the launch traced here: 319 us
  waiting for transfers between devices  184 us (58%)
  blocking collectives  63.7 us (20%)
  matrix products  27 us (8%)
  between operations  14.1 us (4%)
  local copies, waits for them, and re-layouts  12 us (4%)
  other arithmetic  10.4 us (3%)
  starting transfers between devices  8.4 us (3%)
    all_gather x1, waiting for transfers between devices, body(): w_head = lax.all_gather(kv_weight, ('pz', 'pc'), axis=1, tiled=True)  92.3 us
    all_gather x1, waiting for transfers between devices, body(): w_all = lax.all_gather(w_head, 'px', axis=1, tiled=True)  65.3 us
    all_to_all x1, blocking collectives, body(): received = lax.all_to_all(jnp.stack(pieces), 'pz', 0, 0)  49.4 us
    reduce_scatter x1, waiting for transfers between devices, body(): lax.psum_scatter(partial_kv.astype(jnp.bfloat16), 'tp', scatter_dimension...  22.6 us
    all_to_all x1, blocking collectives, body(): lax.all_to_all(step, ('px', 'pc'), split_axis=1, concat_axis=1, tiled=True)  14.3 us
    dot_general x1, matrix products, body(): jnp.dot(picks, table, preferred_element_type=jnp.float32)  9.18 us
    all_to_all x1, starting transfers between devices, body(): lax.all_to_all(reply, POOL, split_axis=0, concat_axis=0, tiled=True)  8.1 us
    convert_element_type x4, other arithmetic, merge(): weights_now.astype(jnp.bfloat16)  7.79 us
  transfers between devices with their start and end apart: 4, of which 4 were waited for; matrix products, arithmetic and copies ran while one was open for 3% of the time, Pallas kernels for 0%

profile of v1, /device:TPU:58, one launch (start us, length us, event | category | flops | bytes accessed | tf_op | source)
XLA Modules:
  0.0 319.3 jit_solution(3861573533596990268)
XLA Ops:
  7.2 0.0 copy-start
  7.2 0.7 fusion.48
  7.9 0.1 pad_maximum_fusion.1
  8.0 1.1 pad_maximum_fusion
  9.1 0.2 reshape.149
  9.3 0.1 copy.213
  9.4 14.3 %all_to_all.15 = bf16[9,8,16,256]{3,2,0,1:T(8,128)(2,1)S(1)} all-to-all(bf16[9,8,16,256]{3,2,0,1:T(8,128)(2,1)S(1)} %bitcast.153), channel_id=1, replica_groups=mesh['px'=4,'pz'=16,'pc'=2,'tp'=4] {'px','pc'}, dimensions={1} | all-to-all | bytes 1179648 | tf_op jit(solution)/shard_map/all_to_all | solution.py:54
  23.7 0.9 fusion.50
  24.9 49.4 %all_to_all.16 = bf16[16,9,8,1,256]{4,2,1,3,0:T(8,128)(2,1)S(1)} all-to-all(bf16[16,9,8,1,256]{4,2,1,3,0:T(8,128)(2,1)S(1)} %fusion.24), channel_id=1, replica_groups=mesh['px'=4,'pz'=16,'pc'=2,'tp'=4] {'pz'}, dimensions={0} | all-to-all | bytes 1179648 | tf_op jit(solution)/shard_map/all_to_all | solution.py:56
  74.3 0.2 reshape_reshape.3
  74.5 0.6 copy.283
  75.2 0.2 reshape.152
  75.5 0.1 fusion.22
  75.5 0.1 eq.17
  75.6 9.2 %fusion.11 = bf16[8192,256]{1,0:T(8,128)(2,1)} fusion(s32[8192]{0:T(1024)S(1)} %eq.17, bf16[128,8,256]{2,0,1:T(8,128)(2,1)S(1)} %slice.39), kind=kOutput, calls=%fused_computation.19 | convolution fusion | flops 4305453056 | bytes 4751360 | tf_op jit(solution)/shard_map/dot_general | solution.py:68
  84.8 0.0 copy-start.2
  84.8 0.0 copy-start.1
  84.8 8.1 %all-to-all-start.2 = ((bf16[128,64,1,256]{3,1,2,0:T(8,128)(2,1)}), bf16[128,64,1,256]{3,1,2,0:T(8,128)(2,1)}, u32[]{:S(2)}, u32[]{:S(2)}) async-start(bf16[128,64,1,256]{3,1,2,0:T(8,128)(2,1)} %bitcast.151), calls=%async_computation.3 | async-start | bytes 8388608 | tf_op jit(solution)/shard_map/all_to_all | solution.py:71
  92.9 0.0 all-gather.3.cloned.1.call-start
  93.0 0.7 all-gather.3.cloned.1.call-update
  93.6 0.0 all-gather.5.cloned.1.call-start
  93.7 92.3 %all-gather.3.cloned.1.call-done = bf16[2048,256]{0,1:T(8,128)(2,1)} async-done(((bf16[2048,8]{0,1:T(8,128)(2,1)}), bf16[2048,256]{0,1:T(8,128)(2,1)}) %all-gather.3.cloned.1.call-update) | async-done | bytes 1048592 | tf_op jit(solution)/shard_map/all_gather | solution.py:72
  186.0 0.0 all-gather.5.cloned.1.call-update
  186.0 0.2 reduce-scatter.2.cloned.1.call-start
  186.3 65.3 %all-gather.5.cloned.1.call-done = bf16[2048,1024]{0,1:T(8,128)(2,1)} async-done(((bf16[2048,256]{0,1:T(8,128)(2,1)}), bf16[2048,1024]{0,1:T(8,128)(2,1)}) %all-gather.5.cloned.1.call-update) | async-done | bytes 4194320 | tf_op jit(solution)/shard_map/all_gather | solution.py:73
  251.5 0.0 copy-done
  251.5 4.4 %convolution_convert_fusion = bf16[128,1024]{1,0:T(8,128)(2,1)} fusion(bf16[128,2048]{1,0:T(8,128)(2,1)S(1)} %copy-done, bf16[2048,1024]{0,1:T(8,128)(2,1)} %all-gather.5.cloned.1.call-done), kind=kOutput, calls=%fused_computation.22 | convolution fusion | flops 537001984 | bytes 4980736 | tf_op jit(solution)/shard_map/dot_general | solution.py:74
  255.9 0.0 reduce-scatter.2.cloned.1.call-update
  255.9 0.0 copy-done.2
  256.0 3.0 gather_fusion
  259.0 0.2 broadcast_select_fusion
  259.2 0.2 copy.212
  259.4 0.0 copy-done.1
  259.5 0.1 reshape_squeeze_reshape.3
  259.6 22.6 %reduce-scatter.2.cloned.1.call-done = bf16[128,256]{1,0:T(8,128)(2,1)} async-done(((bf16[128,1024]{1,0:T(8,128)(2,1)}), bf16[128,256]{1,0:T(8,128)(2,1)}) %reduce-scatter.2.cloned.1.call-update) | async-done | bytes 65552 | tf_op jit(solution)/shard_map/reduce_scatter | solution.py:75
  282.2 1.0 select_reduce_fusion
  283.2 0.1 fusion.16
  283.3 1.0 fusion.17
  284.4 2.8 all-to-all-done.2
  287.2 24.6 %while.15 = (s32[]{:T(128)}, f32[1024]{0:T(1024)S(1)}, f32[1024]{0:T(1024)S(1)}, f32[1024,128]{1,0:T(8,128)S(1)}, bf16[4,2048,256]{2,1,0:T(8,128)(2,1)}, /*index...) while((s32[]{:T(128)}, f32[1024]{0:T(1024)S(1)}, f32[1024]{0:T(1024)S(1)}, ...), condition=%wide.region_6.7_spmd.clone, body=%wide.region_3.6_spmd.clone.sunk | while | flops 1090783232 | bytes 29814880 | solution.py:104
  287.2 1.3 dynamic-slice_bitcast_fusion.2
  288.5 1.3 fusion.64
  289.8 1.9 fusion.65
  291.8 1.5 convolution_add_fusion.2
  293.3 1.3 dynamic-slice_bitcast_fusion.2
  294.6 1.3 fusion.64
  295.9 1.9 fusion.65
  297.9 1.5 convolution_add_fusion.2
  299.5 1.3 dynamic-slice_bitcast_fusion.2
  300.8 1.3 fusion.64
  302.1 1.9 fusion.65
  304.1 1.5 convolution_add_fusion.2
  305.6 1.3 dynamic-slice_bitcast_fusion.2
  306.9 1.3 fusion.64
  308.3 1.9 fusion.65
  310.2 1.5 convolution_add_fusion.2
  311.8 0.2 divide_convert_fusion
  312.0 0.8 convert_element_type.43
  (37 shorter events, 0.3 us)
Async XLA Ops:
  7.2 244.4 %copy-start = (bf16[128,2048]{1,0:T(8,128)(2,1)S(1)}, bf16[128,2048]{1,0:T(8,128)(2,1)}, u32[]{:S(2)}) copy-start(bf16[128,2048]{1,0:T(8,128)(2,1)} %param.8) | copy-start | bytes 1572868
  84.8 171.2 %copy-start.2 = (s32[1,2,64]{2,1,0:T(2,128)S(1)}, s32[1,2,64]{2,1,0:T(2,128)}, u32[]{:S(2)}) copy-start(s32[1,2,64]{2,1,0:T(2,128)} %param.13) | copy-start | bytes 1540
  84.8 174.6 %copy-start.1 = (bf16[128,1024]{1,0:T(8,128)(2,1)S(1)}, bf16[128,1024]{1,0:T(8,128)(2,1)}, u32[]{:S(2)}) copy-start(bf16[128,1024]{1,0:T(8,128)(2,1)} %param.10) | copy-start | bytes 786436
  84.8 202.4 %all-to-all-start.2 = ((bf16[128,64,1,256]{3,1,2,0:T(8,128)(2,1)}), bf16[128,64,1,256]{3,1,2,0:T(8,128)(2,1)}, u32[]{:S(2)}, u32[]{:S(2)}) async-start(bf16[128,64,1,256]{3,1,2,0:T(8,128)(2,1)} %bitcast.151), calls=%async_computation.3 | async-start | bytes 8388608 | tf_op jit(solution)/shard_map/all_to_all | solution.py:71
  92.9 93.1 %all-gather.3.cloned.1.call-start = ((), (), s32[]{:S(2)}) async-start(), calls=%async_computation.4 | async-start | bytes 1081344 | tf_op jit(solution)/shard_map/all_gather | solution.py:72
  93.6 157.9 %all-gather.5.cloned.1.call-start = ((), (), s32[]{:S(2)}) async-start(), calls=%async_computation.5 | async-start | bytes 5242880 | tf_op jit(solution)/shard_map/all_gather | solution.py:73
  186.0 96.2 %reduce-scatter.2.cloned.1.call-start = ((), (), s32[]{:S(2)}) async-start(), calls=%async_computation.6 | async-start | bytes 327680 | tf_op jit(solution)/shard_map/reduce_scatter | solution.py:75
Sparse Core Ops, SparseCore 0:
  95.9 90.0 all-gather.2
  188.1 63.4 all-gather.4
  256.1 26.0 reduce-scatter.1
